TPU v7x, 256 devices: a whole 4x4x8 slice. The times are simulated.
256 devices in a mesh: blk: 8 (over x, core), dev: 32 (over z, y).
Axes of the slice: x: 4, y: 4, z: 8, core: 2. Of those that a mesh axis runs over, the one named last changes fastest.
Arguments:
- echoes: bfloat16 [2, 4, 2048, 16384], P(None, None, ('blk', 'dev')), may hold values from -6 to 6
- range_phase: float32 [16384], replicated, may hold values from -3.140625 to 3.140625
- offsets: int32 [16384], P('dev'), may hold values from 0 to 56, as said below
- tap_weights: float32 [8, 384], replicated, may hold values from -2 to 2
- channel_mix: float32 [2, 4, 4, 384], replicated, may hold values from -2 to 2
- azimuth_filter: float32 [2, 4, 384], replicated, may hold values from -4 to 4
Outputs:
- focused_image: bfloat16 [2, 4, 2048, 16384], P(None, None, 'blk', 'dev')
Inputs may be any that keep to these rules, and one draw needn't show every extreme that they name: `offsets`: each range bin's offset lies between 0 and 56; some range bin has exactly 56.
All inputs are finite; a program needn't handle non-finite values.
Results may differ from a plain program's by a relative error of at most 0.0088.
Values may be sent and summed in bfloat16 or wider, within the bound.
No kernel may reach another device: no remote copies, remote signals or barrier semaphores. Data moves between devices by JAX's collectives and lax.ppermute only.
A program may use at most 128 MiB of HBM per device.

v0:
```python
import math
import jax
import jax.numpy as jnp
from jax import lax
from jax.sharding import PartitionSpec as P

R1 = 128
MARG = 64


def shifted(block, axis, distance):
    devices = range(lax.axis_size(axis))
    route = [(i - distance, i) for i in devices if i - distance in devices]
    return lax.ppermute(block, axis, route)


def phase_pair(row_count, col_count, length, direction, factor):
    product = (
        jnp.arange(row_count, dtype=jnp.int32)[:, None]
        * jnp.arange(col_count, dtype=jnp.int32)[None, :]
        % length
    )
    angle = product.astype(jnp.float32) * (direction * 2.0 * math.pi / length)
    return (jnp.cos(angle) * factor, jnp.sin(angle) * factor)


def complex_table(row_count, col_count, length, direction, factor):
    cosine, sine = phase_pair(row_count, col_count, length, direction, factor)
    upper = jnp.stack([cosine, -sine], axis=1)
    lower = jnp.stack([sine, cosine], axis=1)
    return jnp.stack([upper, lower]).astype(jnp.bfloat16)


def apply_table(table, data, part_dim, index_dim):
    return lax.dot_general(
        table, data, (((2, 3), (part_dim, index_dim)), ((), ())), preferred_element_type=jnp.float32
    )


def compress(echoes, range_phase):
    cosine = jnp.cos(range_phase)
    sine = jnp.sin(range_phase)
    real_in = echoes[0].astype(jnp.float32)
    imag_in = echoes[1].astype(jnp.float32)
    spectrum = jnp.stack(
        [real_in * cosine - imag_in * sine, real_in * sine + imag_in * cosine]
    ).astype(jnp.bfloat16)
    channels = spectrum.shape[1]
    pulses = spectrum.shape[2]
    range_bins = spectrum.shape[3]
    second = range_bins // R1
    spectrum = spectrum.reshape((2, channels, pulses, R1, second))
    section = apply_table(complex_table(R1, R1, R1, 1.0, 1.0), spectrum, 0, 3)
    twist_re, twist_im = phase_pair(R1, second, range_bins, 1.0, 1.0 / math.sqrt(range_bins))
    twist_re = twist_re[:, None, None, :]
    twist_im = twist_im[:, None, None, :]
    partial_terms = jnp.stack(
        [
            section[0] * twist_re - section[1] * twist_im,
            section[0] * twist_im + section[1] * twist_re,
        ]
    ).astype(jnp.bfloat16)
    result = apply_table(
        complex_table(second, second, second, 1.0, 1.0), partial_terms, 0, 4
    ).astype(jnp.bfloat16)
    return result.transpose(0, 3, 4, 1, 2).reshape((2, channels, pulses, range_bins))


def doppler(window):
    wide = window.shape[2]
    forward = complex_table(wide, wide, wide, -1.0, 1.0 / math.sqrt(wide))
    return apply_table(forward, window, 0, 2).astype(jnp.bfloat16)


def migrate(extended, offsets, tap_weights, block):
    tile = min(128, block)
    taps = tap_weights.shape[0]
    pieces = []
    for tile_index in range(block // tile):
        first = tile_index * tile
        rows_here = jnp.arange(tile, dtype=jnp.int32)
        target = rows_here + offsets[first : first + tile]
        columns = jnp.arange(tile + MARG, dtype=jnp.int32)
        tap_range = jnp.arange(taps, dtype=jnp.int32)
        onehot = (
            columns[None, None, :] == target[None, :, None] + tap_range[:, None, None]
        ).astype(jnp.bfloat16)
        window_part = extended[:, :, :, first : first + tile + MARG]
        picked = lax.dot_general(
            window_part, onehot, (((3,), (2,)), ((), ())), preferred_element_type=jnp.float32
        )
        total = jnp.zeros(picked.shape[:3] + (tile,), jnp.float32)
        for tap_index in range(taps):
            total = total + picked[:, :, :, tap_index] * tap_weights[tap_index][None, :, None, None]
        pieces.append(total)
    return jnp.concatenate(pieces, axis=3)


def body(echoes, range_phase, offsets, tap_weights, channel_mix, azimuth_filter):
    dev_count = lax.axis_size("dev")
    compressed = compress(echoes, range_phase)
    range_bins = compressed.shape[3]
    block = range_bins // dev_count
    turned = lax.all_to_all(compressed, "dev", split_axis=3, concat_axis=2, tiled=True)
    group_pulses = turned.shape[2]
    intersection = group_pulses // 2
    following = shifted(turned[:, :, :intersection], "blk", -1)
    spectra = doppler(jnp.concatenate([turned, following], axis=2))
    border = shifted(spectra[:, :, :, :MARG], "dev", -1)
    extended = jnp.concatenate([spectra, border], axis=3)
    wide = extended.shape[1]
    channels = extended.shape[2]
    moved = migrate(extended, offsets, tap_weights, block)
    mix_real = (
        azimuth_filter[0][:, None, :] * channel_mix[0]
        - azimuth_filter[1][:, None, :] * channel_mix[1]
    )
    mix_imag = (
        azimuth_filter[0][:, None, :] * channel_mix[1]
        + azimuth_filter[1][:, None, :] * channel_mix[0]
    )
    rows_real = []
    rows_imag = []
    for channel in range(channels):
        sum_real = jnp.zeros((wide, block), jnp.float32)
        sum_imag = jnp.zeros((wide, block), jnp.float32)
        for other_chan in range(channels):
            coef_real = mix_real[channel, other_chan][:, None]
            coef_imag = mix_imag[channel, other_chan][:, None]
            sum_real = (
                sum_real + coef_real * moved[0, :, other_chan] - coef_imag * moved[1, :, other_chan]
            )
            sum_imag = (
                sum_imag + coef_real * moved[1, :, other_chan] + coef_imag * moved[0, :, other_chan]
            )
        rows_real.append(sum_real)
        rows_imag.append(sum_imag)
    focused = jnp.stack([jnp.stack(rows_real, axis=1), jnp.stack(rows_imag, axis=1)]).astype(
        jnp.bfloat16
    )
    backward = complex_table(group_pulses, wide, wide, 1.0, 1.0 / math.sqrt(wide))
    image = apply_table(backward, focused, 0, 1).astype(jnp.bfloat16)
    return image.transpose(0, 2, 1, 3)


def solution(mesh):
    in_specs = (P(None, None, ("blk", "dev"), None), P(), P("dev"), P(), P(), P())
    out_specs = P(None, None, "blk", "dev")
    return jax.shard_map(body, mesh=mesh, in_specs=in_specs, out_specs=out_specs, check_vma=False)
```

profile of v0, /device:TPU:35, one launch (start us, length us, event | category | flops | bytes accessed | tf_op | source)
XLA Modules:
  0.0 278.3 jit_solution(915196148581060619)
XLA Ops:
  1.9 2.2 fusion.88
  6.8 24.4 %copy.105 = bf16[2,4,8,128,128]{2,1,0,4,3:T(4,128)(2,1)} copy(bf16[2,4,8,128,128]{4,3,2,1,0:T(8,128)(2,1)S(1)} %fusion.15) | data formatting | bytes 4194304 | tf_op jit(solution)/shard_map/reshape | solution.py:66
  31.2 39.5 %reshape.3041 = bf16[32,2,16384]{2,1,0:T(2,128)(2,1)} reshape(bf16[16384,2,4,8]{3,2,1,0:T(4,128)(2,1)} %bitcast.547) | data formatting | bytes 4194304
  70.8 10.9 %all-to-all-start = ((bf16[32,2,16384]{2,1,0:T(2,128)(2,1)}), bf16[32,2,16384]{2,1,0:T(2,128)(2,1)S(1)}, u32[]{:S(2)}, u32[]{:S(2)}) async-start(bf16[32,2,16384]{2,1,0:T(2,128)(2,1)} %reshape.3041), calls=%async_computation | async-start | bytes 4194304 | tf_op jit(solution)/shard_map/all_to_all | solution.py:104
  84.7 2.3 fusion.106
  88.7 2.6 negate_convert_fusion
  92.2 36.5 %all-to-all-done = bf16[32,2,16384]{2,1,0:T(2,128)(2,1)S(1)} async-done(((bf16[32,2,16384]{2,1,0:T(2,128)(2,1)}), bf16[32,2,16384]{2,1,0:T(2,128)(2,1)S(1)}, u32[]{:S(2)}, u32[]{:S(2)}) %all-to-all-start) | async-done | bytes 2097184 | tf_op jit(solution)/shard_map/all_to_all | solution.py:104
  128.6 40.6 %reshape.3042 = bf16[16384,2,4,8]{3,2,1,0:T(4,128)(2,1)} reshape(bf16[32,2,16384]{2,1,0:T(2,128)(2,1)S(1)} %all-to-all-done) | data formatting | bytes 4194304
  169.2 40.2 %copy.47 = bf16[2,4,8,32,512]{4,2,3,0,1:T(8,128)(2,1)S(1)} copy(bf16[2,4,8,32,512]{2,1,0,4,3:T(4,128)(2,1)} %bitcast.548) | data formatting | bytes 4194304 | tf_op jit(solution)/shard_map/all_to_all | solution.py:104
  209.6 6.1 %collective-permute-start = (bf16[2,4,128,512]{3,2,0,1:T(8,128)(2,1)S(1)}, bf16[2,4,128,512]{3,2,0,1:T(8,128)(2,1)S(1)}, u32[]{:S(2)}, u32[]{:S(2)}) collective-permute-start(bf16[2,4,128,512]{3,2,0,1:T(8,128)(2,1)S(1)} %slice.481), channel_id=1, source_target_pairs={{32,0},{64,32},{96,64},{128,96},{160,128},{192,160},{224,192},{33,... | collective-permute-start | bytes 3145736 | tf_op jit(solution)/shard_map/ppermute | solution.py:14
  217.1 11.9 %collective-permute-done = bf16[2,4,128,512]{3,2,0,1:T(8,128)(2,1)S(1)} collective-permute-done((bf16[2,4,128,512]{3,2,0,1:T(8,128)(2,1)S(1)}, bf16[2,4,128,512]{3,2,0,1:T(8,128)(2,1)S(1)}, u32[]{:S(2)}, u32[]{:S(2)}) %collective-permute-start) | collective-permute-done | bytes 1048608 | tf_op jit(solution)/shard_map/ppermute | solution.py:14
  229.0 4.4 %bitcast_convert_fusion = bf16[2,384,4,512]{3,1,2,0:T(8,128)(2,1)S(1)} fusion(bf16[2,4,128,512]{3,2,0,1:T(8,128)(2,1)S(1)} %collective-permute-done, bf16[2,4,256,512]{3,2,0,1:T(8,128)(2,1)} %bitcast.550, bf16[1,384,2,384]{3,1,2,0:T(8,128)(2,1)S(1)} %get-tuple-element.50, bf16[1,384,2,384]{3,1,2,0:T(8,128)(2,1)S(1)} %get-tuple-element.49), kind=kOutput, calls=%fused_computation.1 | convolution fusion | flops 2426142720 | bytes 7471104 | tf_op jit(solution)/shard_map/dot_general | solution.py:35
  234.5 2.1 copy.74
  236.6 4.4 %collective-permute-start.1 = (bf16[2,384,4,64]{1,3,2,0:T(8,128)(2,1)}, bf16[2,384,4,64]{1,3,2,0:T(8,128)(2,1)}, u32[]{:S(2)}, u32[]{:S(2)}) collective-permute-start(bf16[2,384,4,64]{1,3,2,0:T(8,128)(2,1)} %copy.74), channel_id=1, source_target_pairs={{1,0},{2,1},{3,2},{4,3},{5,4},{6,5},{7,6},{8,7},{9,8},{10,9},{11,1... | collective-permute-start | bytes 1179656 | tf_op jit(solution)/shard_map/ppermute | solution.py:14
  241.1 1.8 fusion.52
  242.9 1.8 fusion.68
  244.9 6.4 %fusion.84 = f32[2,384,4,8,128]{1,4,3,2,0:T(8,128)} fusion(bf16[2,384,4,512]{3,1,2,0:T(8,128)(2,1)S(1)} %bitcast_convert_fusion, s32[8,128]{1,0:T(8,128)S(1)} %copy-done.51), kind=kOutput, calls=%fused_computation.132 | convolution fusion | flops 1208156160 | bytes 14159872 | tf_op jit(solution)/shard_map/dot_general | solution.py:89
  251.3 2.3 fusion.38
  253.6 2.3 fusion.54
  255.9 2.8 %copy-done = f32[2,384,4,8,128]{1,4,3,2,0:T(8,128)S(1)} copy-done((f32[2,384,4,8,128]{1,4,3,2,0:T(8,128)S(1)}, f32[2,384,4,8,128]{1,4,3,2,0:T(8,128)}, u32[]{:S(2)}) %copy-start) | copy-done | bytes 12582936
  258.7 2.3 fusion.70
  261.0 2.2 copy.75
  263.2 3.0 %fusion.34 = f32[2,384,4,8,128]{1,4,2,0,3:T(8,128)S(1)} fusion(bf16[2,384,4,64]{3,1,2,0:T(8,128)(2,1)} %copy.75, bf16[2,384,4,512]{3,1,2,0:T(8,128)(2,1)S(1)} %bitcast_convert_fusion, s32[8,128]{1,0:T(8,128)S(1)} %iota_add_fusion), kind=kOutput, calls=%fused_computation.56 | convolution fusion | flops 1210515456 | bytes 16125952 | tf_op jit(solution)/shard_map/dot_general | solution.py:89
  275.1 3.1 %fusion.10 = bf16[2,4,256,512]{3,2,1,0:T(8,128)(2,1)} fusion(bf16[1,384,4,512]{1,3,2,0:T(8,128)(2,1)S(1)} %maximum_bitcast_fusion.11, bf16[1,384,4,512]{1,3,2,0:T(8,128)(2,1)S(1)} %maximum_bitcast_fusion.10, bf16[1,256,2,384]{3,1,2,0:T(8,128)(2,1)S(1)} %copy-done.5, bf16[1,256,2,384]{3,1,2,0:T(8,128)(2,1)S(1)} %get-tuple-element.51), kind=kOutput, calls=%fused_computation.21 | convolution fusion | flops 1619525632 | bytes 6029312 | tf_op jit(solution)/shard_map/dot_general | solution.py:35
  (146 shorter events, 21.1 us)
Async XLA Ops:
  70.8 10.9 %copy-start.53 = (f32[2,4,384]{2,1,0:T(4,128)S(1)}, f32[2,4,384]{2,1,0:T(4,128)}, u32[]{:S(2)}) copy-start(f32[2,4,384]{2,1,0:T(4,128)} %param.11) | copy-start | bytes 36868
  70.8 11.0 %copy-start.18 = (f32[2,4,4,384]{3,2,1,0:T(4,128)S(1)}, f32[2,4,4,384]{3,2,1,0:T(4,128)}, u32[]{:S(2)}) copy-start(f32[2,4,4,384]{3,2,1,0:T(4,128)} %param.10) | copy-start | bytes 147460
  70.8 57.9 %all-to-all-start = ((bf16[32,2,16384]{2,1,0:T(2,128)(2,1)}), bf16[32,2,16384]{2,1,0:T(2,128)(2,1)S(1)}, u32[]{:S(2)}, u32[]{:S(2)}) async-start(bf16[32,2,16384]{2,1,0:T(2,128)(2,1)} %reshape.3041), calls=%async_computation | async-start | bytes 4194304 | tf_op jit(solution)/shard_map/all_to_all | solution.py:104
  209.5 7.0 %copy-start.4 = (bf16[2,4,8,32,512]{4,2,3,0,1:T(8,128)(2,1)}, bf16[2,4,8,32,512]{4,2,3,0,1:T(8,128)(2,1)S(1)}, u32[]{:S(2)}) copy-start(bf16[2,4,8,32,512]{4,2,3,0,1:T(8,128)(2,1)S(1)} %copy.47) | copy-start | bytes 6291460
  209.5 6.2 %copy-start.52 = (f32[8,384]{1,0:T(8,128)S(1)}, f32[8,384]{1,0:T(8,128)}, u32[]{:S(2)}) copy-start(f32[8,384]{1,0:T(8,128)} %param.9) | copy-start | bytes 36868
  209.5 7.0 %copy-start.54 = (s32[512]{0:T(512)S(1)}, s32[512]{0:T(512)}, u32[]{:S(2)}) copy-start(s32[512]{0:T(512)} %param.8) | copy-start | bytes 6148
  209.6 19.4 %collective-permute-start = (bf16[2,4,128,512]{3,2,0,1:T(8,128)(2,1)S(1)}, bf16[2,4,128,512]{3,2,0,1:T(8,128)(2,1)S(1)}, u32[]{:S(2)}, u32[]{:S(2)}) collective-permute-start(bf16[2,4,128,512]{3,2,0,1:T(8,128)(2,1)S(1)} %slice.481), channel_id=1, source_target_pairs={{32,0},{64,32},{96,64},{128,96},{160,128},{192,160},{224,192},{33,... | collective-permute-start | bytes 3145736 | tf_op jit(solution)/shard_map/ppermute | solution.py:14
  236.6 24.4 %collective-permute-start.1 = (bf16[2,384,4,64]{1,3,2,0:T(8,128)(2,1)}, bf16[2,384,4,64]{1,3,2,0:T(8,128)(2,1)}, u32[]{:S(2)}, u32[]{:S(2)}) collective-permute-start(bf16[2,384,4,64]{1,3,2,0:T(8,128)(2,1)} %copy.74), channel_id=1, source_target_pairs={{1,0},{2,1},{3,2},{4,3},{5,4},{6,5},{7,6},{8,7},{9,8},{10,9},{11,1... | collective-permute-start | bytes 1179656 | tf_op jit(solution)/shard_map/ppermute | solution.py:14
  242.9 1.9 copy-start.51
  244.8 6.5 %copy-start.6 = (f32[384]{0:T(512)S(1)}, f32[384]{0:T(512)}, u32[]{:S(2)}) copy-start(f32[384]{0:T(512)} %get-tuple-element.38) | copy-start | bytes 4612
  244.8 6.5 %copy-start.7 = (f32[384]{0:T(512)S(1)}, f32[384]{0:T(512)}, u32[]{:S(2)}) copy-start(f32[384]{0:T(512)} %get-tuple-element.39) | copy-start | bytes 4612
  244.8 6.5 %copy-start.8 = (f32[384]{0:T(512)S(1)}, f32[384]{0:T(512)}, u32[]{:S(2)}) copy-start(f32[384]{0:T(512)} %get-tuple-element.40) | copy-start | bytes 4612
  244.8 6.5 %copy-start.10 = (f32[384]{0:T(512)S(1)}, f32[384]{0:T(512)}, u32[]{:S(2)}) copy-start(f32[384]{0:T(512)} %get-tuple-element.41) | copy-start | bytes 4612
  244.8 6.5 %copy-start.12 = (f32[384]{0:T(512)S(1)}, f32[384]{0:T(512)}, u32[]{:S(2)}) copy-start(f32[384]{0:T(512)} %get-tuple-element.42) | copy-start | bytes 4612
  244.8 6.5 %copy-start.14 = (f32[384]{0:T(512)S(1)}, f32[384]{0:T(512)}, u32[]{:S(2)}) copy-start(f32[384]{0:T(512)} %get-tuple-element.43) | copy-start | bytes 4612
  244.8 6.5 %copy-start.16 = (f32[384]{0:T(512)S(1)}, f32[384]{0:T(512)}, u32[]{:S(2)}) copy-start(f32[384]{0:T(512)} %get-tuple-element.44) | copy-start | bytes 4612
  253.6 5.1 %copy-start = (f32[2,384,4,8,128]{1,4,3,2,0:T(8,128)S(1)}, f32[2,384,4,8,128]{1,4,3,2,0:T(8,128)}, u32[]{:S(2)}) copy-start(f32[2,384,4,8,128]{1,4,3,2,0:T(8,128)} %fusion.84) | copy-start | bytes 37748740
  263.2 3.0 %copy-start.9 = (f32[384]{0:T(512)S(1)}, f32[384]{0:T(512)}, u32[]{:S(2)}) copy-start(f32[384]{0:T(512)} %get-tuple-element.40) | copy-start | bytes 4612
  263.2 3.0 %copy-start.11 = (f32[384]{0:T(512)S(1)}, f32[384]{0:T(512)}, u32[]{:S(2)}) copy-start(f32[384]{0:T(512)} %get-tuple-element.41) | copy-start | bytes 4612
  263.2 3.0 %copy-start.13 = (f32[384]{0:T(512)S(1)}, f32[384]{0:T(512)}, u32[]{:S(2)}) copy-start(f32[384]{0:T(512)} %get-tuple-element.42) | copy-start | bytes 4612
  263.2 3.0 %copy-start.15 = (f32[384]{0:T(512)S(1)}, f32[384]{0:T(512)}, u32[]{:S(2)}) copy-start(f32[384]{0:T(512)} %get-tuple-element.43) | copy-start | bytes 4612
  263.2 3.0 %copy-start.17 = (f32[384]{0:T(512)S(1)}, f32[384]{0:T(512)}, u32[]{:S(2)}) copy-start(f32[384]{0:T(512)} %get-tuple-element.44) | copy-start | bytes 4612
  266.3 1.9 copy-start.2
  266.3 2.3 copy-start.3
  (34 other events, 24.8 us)
where the time goes:
time: 281 us; the launch traced here: 278 us
  local copies, waits for them, and re-layouts  159 us (57%)
  waiting for transfers between devices  48.4 us (17%)
  other arithmetic  26.1 us (9%)
  matrix products  22.1 us (8%)
  starting transfers between devices  21.4 us (8%)
    unnamed x112, local copies, waits for them, and re-layouts  85.8 us
    all_to_all x1, local copies, waits for them, and re-layouts, body(): lax.all_to_all(compressed, 'dev', split_axis=3, concat_axis=2, tiled=True)  40.2 us
    all_to_all x1, waiting for transfers between devices, body(): lax.all_to_all(compressed, 'dev', split_axis=3, concat_axis=2, tiled=True)  36.5 us
    reshape x1, local copies, waits for them, and re-layouts, compress(): result.transpose(0, 3, 4, 1, 2).reshape((2, channels, pulses, range_bins))  24.4 us
    dot_general x4, matrix products, migrate(): lax.dot_general(window_part, onehot, (((3,), (2,)), ((), ())), preferred_...  13.1 us
    another operation x15, other arithmetic  12.8 us
    ppermute x2, waiting for transfers between devices, shifted(): return lax.ppermute(block, axis, route)  11.9 us
    all_to_all x1, starting transfers between devices, body(): lax.all_to_all(compressed, 'dev', split_axis=3, concat_axis=2, tiled=True)  10.9 us
  transfers between devices with their start and end apart: 3, of which 2 were waited for; matrix products, arithmetic and copies ran while one was open for 10% of the time, Pallas kernels for 0%

commit v1 on v0

--- a/solution.py
+++ b/solution.py
@@ -101,7 +101,10 @@
     compressed = compress(echoes, range_phase)
     range_bins = compressed.shape[3]
     block = range_bins // dev_count
-    turned = lax.all_to_all(compressed, "dev", split_axis=3, concat_axis=2, tiled=True)
+    turned = jnp.concatenate(
+        lax.all_to_all(jnp.stack(jnp.split(compressed, lax.axis_size("dev"), axis=3)), "dev", 0, 0),
+        axis=2,
+    )
     group_pulses = turned.shape[2]
     intersection = group_pulses // 2
     following = shifted(turned[:, :, :intersection], "blk", -1)

time: 281 us -> 157 us (0.56)
  local copies, waits for them, and re-layouts: 159 us -> 37.9 us
    unnamed x112 -> x139, local copies, waits for them, and re-layouts: 85.8 us -> 25.2 us
    all_to_all x1 -> x0, local copies, waits for them, and re-layouts: 40.2 us -> none  [body(): lax.all_to_all(compressed, 'dev', split_axis=3, concat_axis=2, tiled=True)]
    reshape x1, local copies, waits for them, and re-layouts: 24.4 us -> 2.82 us  [compress(): result.transpose(0, 3, 4, 1, 2).reshape((2, channels, pulses, range_bins))]
  transfers between devices with their start and end apart: 3 -> 3, of which waited for: 2 -> 2; matrix products, arithmetic and copies ran while one was open for 10% -> 18% of each run, Pallas kernels for 0% -> 0%
where the time goes in v1:
time: 157 us
  waiting for transfers between devices  48.6 us (31%)
  local copies, waits for them, and re-layouts  37.9 us (24%)
  other arithmetic  26.1 us (17%)
  matrix products  21.9 us (14%)
  starting transfers between devices  21.4 us (14%)
    all_to_all x1, waiting for transfers between devices, body(): lax.all_to_all(jnp.stack(jnp.split(compressed, lax.axis_size('dev'), axis...  36.5 us
    unnamed x139, local copies, waits for them, and re-layouts  25.2 us
    dot_general x4, matrix products, migrate(): lax.dot_general(window_part, onehot, (((3,), (2,)), ((), ())), preferred_...  13.1 us
    another operation x15, other arithmetic  12.8 us
    ppermute x2, waiting for transfers between devices, shifted(): return lax.ppermute(block, axis, route)  12.2 us
    all_to_all x1, starting transfers between devices, body(): lax.all_to_all(jnp.stack(jnp.split(compressed, lax.axis_size('dev'), axis...  10.9 us
    ppermute x2, starting transfers between devices, shifted(): return lax.ppermute(block, axis, route)  10.5 us
    dot_general x4, matrix products, apply_table(): lax.dot_general(table, data, (((2, 3), (part_dim, index_dim)), ((), ())),...  8.78 us
  transfers between devices with their start and end apart: 3, of which 2 were waited for; matrix products, arithmetic and copies ran while one was open for 18% of the time, Pallas kernels for 0%

profile of v1, /device:TPU:35, one launch (start us, length us, event | category | flops | bytes accessed | tf_op | source)
XLA Modules:
  0.0 156.7 jit_solution(14900577113274204156)
XLA Ops:
  1.9 2.2 %fusion.88 = (bf16[4,8,128,128]{3,1,2,0:T(8,128)(2,1)S(1)}, bf16[4,8,128,128]{3,1,2,0:T(8,128)(2,1)S(1)}) fusion(f32[16384]{0:T(1024)S(1)} %get-tuple-element.54, f32[16384]{0:T(1024)S(1)} %get-tuple-element.53, bf16[2,4,8,16384]{3,2,1,0:T(8,128)(2,1)} %param.6), kind=kLoop, calls=%fused_computation.140 | loop fusion | flops 5242880 | bytes 4325376
  6.1 2.1 %fusion.15 = bf16[2,4,8,128,128]{4,3,2,1,0:T(8,128)(2,1)} fusion(bf16[1,128,2,128]{3,1,2,0:T(8,128)(2,1)S(1)} %get-tuple-element.58, bf16[1,128,2,128]{3,1,2,0:T(8,128)(2,1)S(1)} %get-tuple-element.57, bf16[1,128,4,8,128]{4,1,3,2,0:T(8,128)(2,1)S(1)} %get-tuple-element.46, bf16[1,128,4,8,128]{4,1,3,2,0:T(8,128)(2,1)S(1)} %get-tuple-element.45), kind=kOutput, calls=%fused_computation.31 | convolution fusion | flops 539230208 | bytes 4325376 | tf_op jit(solution)/shard_map/dot_general | solution.py:35
  8.2 2.8 %reshape.2987 = bf16[2,4,8,16384]{3,2,1,0:T(8,128)(2,1)S(1)} reshape(bf16[2,4,8,128,128]{4,3,2,1,0:T(8,128)(2,1)} %fusion.15) | data formatting | bytes 4194304 | tf_op jit(solution)/shard_map/reshape | solution.py:66
  31.3 10.9 %all-to-all-start = ((bf16[32,2,4,8,512]{4,3,2,1,0:T(8,128)(2,1)}), bf16[32,2,4,8,512]{4,3,2,1,0:T(8,128)(2,1)S(1)}, u32[]{:S(2)}, u32[]{:S(2)}) async-start(bf16[32,2,4,8,512]{4,3,2,1,0:T(8,128)(2,1)} %constant_dynamic-update-slice_fusion), calls=%async_computation | async-start | bytes 4194304 | tf_op jit(solution)/shard_map/all_to_all | solution.py:105
  43.6 1.5 fusion.116
  45.2 2.3 %fusion.106 = bf16[384,1,384]{2,0,1:T(8,128)(2,1)S(1)} fusion(), kind=kLoop, calls=%fused_computation.184 | loop fusion | flops 1622016 | bytes 294912 | tf_op jit(solution)/shard_map/convert.29
  47.5 1.7 %negate_convert_fusion.1 = (bf16[256,1,384]{2,0,1:T(8,128)(2,1)S(1)}, bf16[256,1,384]{2,0,1:T(8,128)(2,1)S(1)}) fusion(), kind=kLoop, calls=%fused_computation.193 | loop fusion | flops 1376256 | bytes 393216 | tf_op jit(solution)/shard_map/convert.41
  49.2 2.6 %negate_convert_fusion = (bf16[384,1,384]{2,0,1:T(8,128)(2,1)S(1)}, bf16[384,1,384]{2,0,1:T(8,128)(2,1)S(1)}) fusion(), kind=kLoop, calls=%fused_computation.177 | loop fusion | flops 2064384 | bytes 589824 | tf_op jit(solution)/shard_map/convert.33
  52.7 36.5 %all-to-all-done = bf16[32,2,4,8,512]{4,3,2,1,0:T(8,128)(2,1)S(1)} async-done(((bf16[32,2,4,8,512]{4,3,2,1,0:T(8,128)(2,1)}), bf16[32,2,4,8,512]{4,3,2,1,0:T(8,128)(2,1)S(1)}, u32[]{:S(2)}, u32[]{:S(2)}) %all-to-all-start) | async-done | bytes 2097184 | tf_op jit(solution)/shard_map/all_to_all | solution.py:105
  89.4 5.9 %collective-permute-start = (bf16[2,4,128,512]{3,2,0,1:T(8,128)(2,1)S(1)}, bf16[2,4,128,512]{3,2,0,1:T(8,128)(2,1)S(1)}, u32[]{:S(2)}, u32[]{:S(2)}) collective-permute-start(bf16[2,4,128,512]{3,2,0,1:T(8,128)(2,1)S(1)} %slice.481), channel_id=1, source_target_pairs={{32,0},{64,32},{96,64},{128,96},{160,128},{192,160},{224,192},{33,... | collective-permute-start | bytes 3145736 | tf_op jit(solution)/shard_map/ppermute | solution.py:14
  96.7 12.2 %collective-permute-done = bf16[2,4,128,512]{3,2,0,1:T(8,128)(2,1)S(1)} collective-permute-done((bf16[2,4,128,512]{3,2,0,1:T(8,128)(2,1)S(1)}, bf16[2,4,128,512]{3,2,0,1:T(8,128)(2,1)S(1)}, u32[]{:S(2)}, u32[]{:S(2)}) %collective-permute-start) | collective-permute-done | bytes 1048608 | tf_op jit(solution)/shard_map/ppermute | solution.py:14
  108.9 2.8 %bitcast_convert_fusion = bf16[2,384,4,512]{3,1,2,0:T(8,128)(2,1)S(1)} fusion(bf16[2,4,128,512]{3,2,0,1:T(8,128)(2,1)S(1)} %collective-permute-done, bf16[2,4,256,512]{3,2,0,1:T(8,128)(2,1)S(1)} %copy_bitcast_fusion, bf16[1,384,2,384]{3,1,2,0:T(8,128)(2,1)S(1)} %get-tuple-element.50, bf16[1,384,2,384]{3,1,2,0:T(8,128)(2,1)S(1)} %get-tuple-element.49), kind=kOutput, calls=%fused_computation.1 | convolution fusion | flops 2426142720 | bytes 7471104 | tf_op jit(solution)/shard_map/dot_general | solution.py:35
  112.7 2.1 %copy.73 = bf16[2,384,4,64]{1,3,2,0:T(8,128)(2,1)} copy(bf16[2,384,4,64]{3,1,2,0:T(8,128)(2,1)} %slice.509) | data formatting | bytes 786432 | tf_op jit(solution)/shard_map/slice | solution.py:112
  114.9 4.6 %collective-permute-start.1 = (bf16[2,384,4,64]{1,3,2,0:T(8,128)(2,1)}, bf16[2,384,4,64]{1,3,2,0:T(8,128)(2,1)}, u32[]{:S(2)}, u32[]{:S(2)}) collective-permute-start(bf16[2,384,4,64]{1,3,2,0:T(8,128)(2,1)} %copy.73), channel_id=1, source_target_pairs={{1,0},{2,1},{3,2},{4,3},{5,4},{6,5},{7,6},{8,7},{9,8},{10,9},{11,1... | collective-permute-start | bytes 1179656 | tf_op jit(solution)/shard_map/ppermute | solution.py:14
  119.5 1.8 %fusion.52 = f32[2,384,4,8,128]{1,4,2,0,3:T(8,128)S(1)} fusion(bf16[2,384,4,512]{3,1,2,0:T(8,128)(2,1)S(1)} %bitcast_convert_fusion, s32[8,128]{1,0:T(8,128)S(1)} %get-tuple-element.73), kind=kOutput, calls=%fused_computation.83 | convolution fusion | flops 1208156160 | bytes 14159872 | tf_op jit(solution)/shard_map/dot_general | solution.py:89
  121.4 1.8 %fusion.68 = f32[2,384,4,8,128]{1,4,2,0,3:T(8,128)S(1)} fusion(bf16[2,384,4,512]{3,1,2,0:T(8,128)(2,1)S(1)} %bitcast_convert_fusion, s32[8,128]{1,0:T(8,128)S(1)} %get-tuple-element.74), kind=kOutput, calls=%fused_computation.108 | convolution fusion | flops 1208156160 | bytes 14159872 | tf_op jit(solution)/shard_map/dot_general | solution.py:89
  123.3 6.4 %fusion.84 = f32[2,384,4,8,128]{1,4,3,2,0:T(8,128)} fusion(bf16[2,384,4,512]{3,1,2,0:T(8,128)(2,1)S(1)} %bitcast_convert_fusion, s32[8,128]{1,0:T(8,128)S(1)} %copy-done.50), kind=kOutput, calls=%fused_computation.133 | convolution fusion | flops 1208156160 | bytes 14159872 | tf_op jit(solution)/shard_map/dot_general | solution.py:89
  129.7 2.3 %fusion.38 = f32[2,384,4,128]{1,3,2,0:T(8,128)} fusion(f32[2,384,4,8,128]{1,4,2,0,3:T(8,128)S(1)} %fusion.52, f32[384]{0:T(512)S(1)} %copy-done.13, f32[384]{0:T(512)S(1)} %copy-done.15, f32[384]{0:T(512)S(1)} %copy-done.5, f32[384]{0:T(512)S(1)} %copy-done.6, f32[384]{0:T(512)S(1)} %copy-done.7, f32[384]{0:T(512)S(1)} %copy-done.9, f32[384]{0:T(512)S(1)} %copy-done.11, ...), kind=kLoop, calls=%fused_computation.61 | loop fusion | flops 5898240 | bytes 14168064 | tf_op jit(solution)/shard_map/add | solution.py:94
  132.0 2.3 %fusion.54 = f32[2,384,4,128]{1,3,2,0:T(8,128)} fusion(f32[2,384,4,8,128]{1,4,2,0,3:T(8,128)S(1)} %fusion.68, f32[384]{0:T(512)S(1)} %copy-done.13, f32[384]{0:T(512)S(1)} %copy-done.15, f32[384]{0:T(512)S(1)} %copy-done.5, f32[384]{0:T(512)S(1)} %copy-done.6, f32[384]{0:T(512)S(1)} %copy-done.7, f32[384]{0:T(512)S(1)} %copy-done.9, f32[384]{0:T(512)S(1)} %copy-done.11, ...), kind=kLoop, calls=%fused_computation.86 | loop fusion | flops 5898240 | bytes 14168064 | tf_op jit(solution)/shard_map/add | solution.py:94
  134.4 2.8 %copy-done = f32[2,384,4,8,128]{1,4,3,2,0:T(8,128)S(1)} copy-done((f32[2,384,4,8,128]{1,4,3,2,0:T(8,128)S(1)}, f32[2,384,4,8,128]{1,4,3,2,0:T(8,128)}, u32[]{:S(2)}) %copy-start) | copy-done | bytes 12582936
  137.2 2.3 %fusion.70 = f32[2,384,4,128]{1,3,2,0:T(8,128)} fusion(f32[2,384,4,8,128]{1,4,3,2,0:T(8,128)S(1)} %copy-done, f32[384]{0:T(512)S(1)} %copy-done.13, f32[384]{0:T(512)S(1)} %copy-done.15, f32[384]{0:T(512)S(1)} %copy-done.5, f32[384]{0:T(512)S(1)} %copy-done.6, f32[384]{0:T(512)S(1)} %copy-done.7, f32[384]{0:T(512)S(1)} %copy-done.9, f32[384]{0:T(512)S(1)} %copy-done.11, ...), kind=kLoop, calls=%fused_computation.111 | loop fusion | flops 5898240 | bytes 14168064 | tf_op jit(solution)/shard_map/add | solution.py:94
  139.5 2.2 %copy.74 = bf16[2,384,4,64]{3,1,2,0:T(8,128)(2,1)} copy(bf16[2,384,4,64]{1,3,2,0:T(8,128)(2,1)} %collective-permute-done.1) | data formatting | bytes 786432 | tf_op jit(solution)/shard_map/ppermute | solution.py:14
  141.6 3.0 %fusion.34 = f32[2,384,4,8,128]{1,4,2,0,3:T(8,128)S(1)} fusion(bf16[2,384,4,64]{3,1,2,0:T(8,128)(2,1)} %copy.74, bf16[2,384,4,512]{3,1,2,0:T(8,128)(2,1)S(1)} %bitcast_convert_fusion, s32[8,128]{1,0:T(8,128)S(1)} %iota_add_fusion), kind=kOutput, calls=%fused_computation.57 | convolution fusion | flops 1210515456 | bytes 16125952 | tf_op jit(solution)/shard_map/dot_general | solution.py:89
  153.5 3.2 %fusion.10 = bf16[2,4,256,512]{3,2,1,0:T(8,128)(2,1)} fusion(bf16[1,384,4,512]{1,3,2,0:T(8,128)(2,1)S(1)} %maximum_bitcast_fusion.11, bf16[1,384,4,512]{1,3,2,0:T(8,128)(2,1)S(1)} %maximum_bitcast_fusion.10, bf16[1,256,2,384]{3,1,2,0:T(8,128)(2,1)S(1)} %copy-done.4, bf16[1,256,2,384]{3,1,2,0:T(8,128)(2,1)S(1)} %get-tuple-element.51), kind=kOutput, calls=%fused_computation.21 | convolution fusion | flops 1619525632 | bytes 6029312 | tf_op jit(solution)/shard_map/dot_general | solution.py:35
  (174 shorter events, 37.5 us)
Async XLA Ops:
  31.3 10.9 %copy-start.52 = (f32[2,4,384]{2,1,0:T(4,128)S(1)}, f32[2,4,384]{2,1,0:T(4,128)}, u32[]{:S(2)}) copy-start(f32[2,4,384]{2,1,0:T(4,128)} %param.11) | copy-start | bytes 36868
  31.3 11.0 %copy-start.17 = (f32[2,4,4,384]{3,2,1,0:T(4,128)S(1)}, f32[2,4,4,384]{3,2,1,0:T(4,128)}, u32[]{:S(2)}) copy-start(f32[2,4,4,384]{3,2,1,0:T(4,128)} %param.10) | copy-start | bytes 147460
  31.3 57.9 %all-to-all-start = ((bf16[32,2,4,8,512]{4,3,2,1,0:T(8,128)(2,1)}), bf16[32,2,4,8,512]{4,3,2,1,0:T(8,128)(2,1)S(1)}, u32[]{:S(2)}, u32[]{:S(2)}) async-start(bf16[32,2,4,8,512]{4,3,2,1,0:T(8,128)(2,1)} %constant_dynamic-update-slice_fusion), calls=%async_computation | async-start | bytes 4194304 | tf_op jit(solution)/shard_map/all_to_all | solution.py:105
  89.3 6.0 %copy-start.51 = (f32[8,384]{1,0:T(8,128)S(1)}, f32[8,384]{1,0:T(8,128)}, u32[]{:S(2)}) copy-start(f32[8,384]{1,0:T(8,128)} %param.9) | copy-start | bytes 36868
  89.3 6.7 %copy-start.53 = (s32[512]{0:T(512)S(1)}, s32[512]{0:T(512)}, u32[]{:S(2)}) copy-start(s32[512]{0:T(512)} %param.8) | copy-start | bytes 6148
  89.4 19.4 %collective-permute-start = (bf16[2,4,128,512]{3,2,0,1:T(8,128)(2,1)S(1)}, bf16[2,4,128,512]{3,2,0,1:T(8,128)(2,1)S(1)}, u32[]{:S(2)}, u32[]{:S(2)}) collective-permute-start(bf16[2,4,128,512]{3,2,0,1:T(8,128)(2,1)S(1)} %slice.481), channel_id=1, source_target_pairs={{32,0},{64,32},{96,64},{128,96},{160,128},{192,160},{224,192},{33,... | collective-permute-start | bytes 3145736 | tf_op jit(solution)/shard_map/ppermute | solution.py:14
  114.9 24.6 %collective-permute-start.1 = (bf16[2,384,4,64]{1,3,2,0:T(8,128)(2,1)}, bf16[2,384,4,64]{1,3,2,0:T(8,128)(2,1)}, u32[]{:S(2)}, u32[]{:S(2)}) collective-permute-start(bf16[2,384,4,64]{1,3,2,0:T(8,128)(2,1)} %copy.73), channel_id=1, source_target_pairs={{1,0},{2,1},{3,2},{4,3},{5,4},{6,5},{7,6},{8,7},{9,8},{10,9},{11,1... | collective-permute-start | bytes 1179656 | tf_op jit(solution)/shard_map/ppermute | solution.py:14
  121.3 1.9 %copy-start.50 = (s32[8,128]{1,0:T(8,128)S(1)}, s32[8,128]{1,0:T(8,128)}, u32[]{:S(2)}) copy-start(s32[8,128]{1,0:T(8,128)} %iota_add_fusion.3) | copy-start | bytes 12292
  123.2 6.5 %copy-start.5 = (f32[384]{0:T(512)S(1)}, f32[384]{0:T(512)}, u32[]{:S(2)}) copy-start(f32[384]{0:T(512)} %get-tuple-element.38) | copy-start | bytes 4612
  123.2 6.5 %copy-start.6 = (f32[384]{0:T(512)S(1)}, f32[384]{0:T(512)}, u32[]{:S(2)}) copy-start(f32[384]{0:T(512)} %get-tuple-element.39) | copy-start | bytes 4612
  123.2 6.5 %copy-start.7 = (f32[384]{0:T(512)S(1)}, f32[384]{0:T(512)}, u32[]{:S(2)}) copy-start(f32[384]{0:T(512)} %get-tuple-element.40) | copy-start | bytes 4612
  123.2 6.5 %copy-start.9 = (f32[384]{0:T(512)S(1)}, f32[384]{0:T(512)}, u32[]{:S(2)}) copy-start(f32[384]{0:T(512)} %get-tuple-element.41) | copy-start | bytes 4612
  123.3 6.5 %copy-start.11 = (f32[384]{0:T(512)S(1)}, f32[384]{0:T(512)}, u32[]{:S(2)}) copy-start(f32[384]{0:T(512)} %get-tuple-element.42) | copy-start | bytes 4612
  123.3 6.5 %copy-start.13 = (f32[384]{0:T(512)S(1)}, f32[384]{0:T(512)}, u32[]{:S(2)}) copy-start(f32[384]{0:T(512)} %get-tuple-element.43) | copy-start | bytes 4612
  123.3 6.5 %copy-start.15 = (f32[384]{0:T(512)S(1)}, f32[384]{0:T(512)}, u32[]{:S(2)}) copy-start(f32[384]{0:T(512)} %get-tuple-element.44) | copy-start | bytes 4612
  132.0 5.1 %copy-start = (f32[2,384,4,8,128]{1,4,3,2,0:T(8,128)S(1)}, f32[2,384,4,8,128]{1,4,3,2,0:T(8,128)}, u32[]{:S(2)}) copy-start(f32[2,384,4,8,128]{1,4,3,2,0:T(8,128)} %fusion.84) | copy-start | bytes 37748740
  141.6 3.0 %copy-start.8 = (f32[384]{0:T(512)S(1)}, f32[384]{0:T(512)}, u32[]{:S(2)}) copy-start(f32[384]{0:T(512)} %get-tuple-element.40) | copy-start | bytes 4612
  141.6 3.0 %copy-start.10 = (f32[384]{0:T(512)S(1)}, f32[384]{0:T(512)}, u32[]{:S(2)}) copy-start(f32[384]{0:T(512)} %get-tuple-element.41) | copy-start | bytes 4612
  141.6 3.0 %copy-start.12 = (f32[384]{0:T(512)S(1)}, f32[384]{0:T(512)}, u32[]{:S(2)}) copy-start(f32[384]{0:T(512)} %get-tuple-element.42) | copy-start | bytes 4612
  141.6 3.0 %copy-start.14 = (f32[384]{0:T(512)S(1)}, f32[384]{0:T(512)}, u32[]{:S(2)}) copy-start(f32[384]{0:T(512)} %get-tuple-element.43) | copy-start | bytes 4612
  141.6 3.0 %copy-start.16 = (f32[384]{0:T(512)S(1)}, f32[384]{0:T(512)}, u32[]{:S(2)}) copy-start(f32[384]{0:T(512)} %get-tuple-element.44) | copy-start | bytes 4612
  144.7 1.4 copy-start.1
  144.7 1.9 %copy-start.2 = (f32[2,384,4,128]{1,3,2,0:T(8,128)S(1)}, f32[2,384,4,128]{1,3,2,0:T(8,128)}, u32[]{:S(2)}) copy-start(f32[2,384,4,128]{1,3,2,0:T(8,128)} %fusion.54) | copy-start | bytes 4718596
  144.7 2.3 %copy-start.3 = (f32[2,384,4,128]{1,3,2,0:T(8,128)S(1)}, f32[2,384,4,128]{1,3,2,0:T(8,128)}, u32[]{:S(2)}) copy-start(f32[2,384,4,128]{1,3,2,0:T(8,128)} %fusion.70) | copy-start | bytes 4718596
  (33 other events, 23.1 us)
